TPU v7x, 256 devices: a whole 4x4x8 slice. The times are simulated.
256 devices in a mesh: blk: 8 (over x, y_lo), grp: 32 (over y_hi, z, core).
Axes of the slice: x: 4, y: 4 (y_hi: 2, y_lo: 2; y = y_hi * 2 + y_lo), z: 8, core: 2. Of those that a mesh axis runs over, the one named last changes fastest.
Arguments:
- centres: float32 [3, 262144], P(None, ('blk', 'grp')), may hold values from -32 to 32, as said below
- coeffs: float32 [3, 262144], P(None, ('blk', 'grp')), may hold values from -2 to 5.5
- residual: float32 [3, 262144], P(None, ('blk', 'grp')), may hold values from -18 to 18
- direction_prev: float32 [3, 262144], P(None, ('blk', 'grp')), may hold values from -6 to 6
- smoothing: float32 [262144], P(('blk', 'grp')), may hold values from 0.5 to 5
- norm_prev: float32 [3], replicated, may hold values from 262144 to 1048576
- support_radius: int32 [1], replicated, may hold values from 900 to 960
- volume_nodes: float32 [3, 262144], P(None, ('blk', 'grp')), may hold values from -34 to 34
- block_lists: int32 [256, 4], P(('blk', 'grp')), may hold values from 0 to 31, as said below
Outputs:
- coeffs_next: float32 [3, 262144], P(None, ('blk', 'grp'))
- residual_next: float32 [3, 262144], P(None, ('blk', 'grp'))
- direction: float32 [3, 262144], P(None, ('blk', 'grp'))
- norm_next: float32 [3], replicated
- displacement: float32 [3, 262144], P(None, ('blk', 'grp'))
Inputs may be any that keep to these rules, and one draw needn't show every extreme that they name: `centres`: every centre of block k has its distance from the z axis within [g, g + 1) with g = k mod 32, and lies at height -0.01 times the square of that distance. `block_lists`: each row names 4 different bands.
All inputs are finite; a program needn't handle non-finite values.
Results may differ from a plain program's by a relative error of at most 0.0003.
Values sent between devices are 32-bit elements; how exact they have to be, the bound alone decides.
No kernel may reach another device: no remote copies, remote signals or barrier semaphores. Data moves between devices by JAX's collectives and lax.ppermute only.
A program may use at most 64 MiB of HBM per device.

v0:
```python
import jax
import jax.numpy as jnp
from jax import lax
from jax.sharding import PartitionSpec as P

RADIUS_UNIT = 0.001


def extended(shard, sides, width):
    for axis, dim in sides:
        size, length = (lax.axis_size(axis), shard.shape[dim])
        up = [(i, (i + 1) % size) for i in range(size - 1)]
        down = [(j, i) for i, j in up]
        last = lax.slice_in_dim(shard, length - width, length, axis=dim)
        leading = lax.slice_in_dim(shard, 0, width, axis=dim)
        before = lax.ppermute(last, axis, up)
        after = lax.ppermute(leading, axis, down)
        shard = jnp.concatenate([before, shard, after], axis=dim)
    return shard


def wendland(sources, targets, radius):
    apart_first = sources[0][:, None] - targets[0][None, :]
    apart_second = sources[1][:, None] - targets[1][None, :]
    apart_third = sources[2][:, None] - targets[2][None, :]
    distance = jnp.sqrt(
        apart_first * apart_first + apart_second * apart_second + apart_third * apart_third
    )
    scaled = distance / radius
    remain = jnp.maximum(1.0 - scaled, 0.0)
    square = remain * remain
    return square * square * (4.0 * scaled + 1.0)


def apply_blocks(total, piece, targets, count, radius):
    blocks = piece.shape[1] // count

    def one(index, carry):
        block = lax.dynamic_slice_in_dim(piece, index * count, count, 1)
        weights = wendland(block[:3], targets, radius)
        return carry + jnp.dot(
            block[3:], weights, preferred_element_type=jnp.float32, precision=lax.Precision.HIGHEST
        )

    return lax.fori_loop(0, blocks, one, total)


def per_device(
    centres,
    coeffs,
    residual,
    direction_prev,
    smoothing,
    norm_prev,
    support_radius,
    volume_nodes,
    block_lists,
):
    radius = support_radius[0].astype(jnp.float32) * RADIUS_UNIT
    count = centres.shape[1]
    scaling = 1.0 + smoothing
    precond = residual / scaling
    norm_now = lax.psum(jnp.sum(residual * precond, axis=1), ("blk", "grp"))
    beta = norm_now / norm_prev
    direction = precond + beta[:, None] * direction_prev
    bundle = jnp.concatenate([centres, direction], axis=0)
    widened = extended(bundle, (("grp", 1),), count)
    kernel_part = apply_blocks(
        jnp.zeros((3, count), jnp.float32),
        lax.all_gather(widened, "blk", axis=1, tiled=True),
        centres,
        count,
        radius,
    )
    image = smoothing * direction + kernel_part
    curvature = lax.psum(jnp.sum(direction * image, axis=1), ("blk", "grp"))
    alpha = norm_now / curvature
    coeffs_next = coeffs + alpha[:, None] * direction
    residual_next = residual - alpha[:, None] * image
    norm_next = lax.psum(jnp.sum(residual_next * residual_next / scaling, axis=1), ("blk", "grp"))
    stacked = jnp.concatenate([centres, coeffs_next], axis=0)
    listed = block_lists[0]
    empty = jnp.zeros((3, volume_nodes.shape[1]), jnp.float32)

    def contribution(carry, block):
        weights = wendland(block[:3], volume_nodes, radius)
        return carry + jnp.dot(
            block[3:], weights, preferred_element_type=jnp.float32, precision=lax.Precision.HIGHEST
        )

    sector_bands = lax.all_gather(stacked, "grp", axis=1, tiled=True)

    def one_entry(carry, band):
        block = lax.dynamic_slice_in_dim(sector_bands, band * count, count, 1)
        return (contribution(carry, block), None)

    displacement, _ = lax.scan(one_entry, empty, listed)
    return (coeffs_next, residual_next, direction, norm_next, displacement)


def solution(mesh):
    placed = (
        P(None, ("blk", "grp")),
        P(None, ("blk", "grp")),
        P(None, ("blk", "grp")),
        P(None, ("blk", "grp")),
        P(("blk", "grp")),
        P(),
        P(),
        P(None, ("blk", "grp")),
        P(("blk", "grp"), None),
    )
    return jax.shard_map(
        per_device,
        mesh=mesh,
        in_specs=placed,
        out_specs=(
            P(None, ("blk", "grp")),
            P(None, ("blk", "grp")),
            P(None, ("blk", "grp")),
            P(),
            P(None, ("blk", "grp")),
        ),
        check_vma=False,
    )
```

profile of v0, /device:TPU:1, one launch (start us, length us, event | category | flops | bytes accessed | tf_op | source)
XLA Modules:
  0.0 473.8 jit_solution(7852668991935339116)
XLA Ops:
  0.6 0.7 broadcast_add_fusion
  1.3 0.8 multiply_reduce_fusion.1
  2.2 81.4 %psum.21 = f32[3]{0:T(128)S(1)} all-reduce(f32[3]{0:T(128)S(1)} %multiply_reduce_fusion.1), channel_id=1, replica_groups=mesh['blk'=8,'grp'=32] {'blk','grp'}, use_global_device_ids=true, to_apply=%region_1.0 | all-reduce | flops 3 | bytes 24 | tf_op jit(solution)/shard_map/psum | solution.py:63
  83.6 0.7 div.42
  84.2 0.8 multiply_add_fusion.2
  85.0 0.7 pad_maximum_fusion.2
  85.8 2.9 collective-permute-start.1
  88.7 2.7 collective-permute-start
  92.4 0.7 pad_maximum_fusion
  93.1 24.6 %all_gather.6 = f32[6,24576]{1,0:T(8,128)S(1)} all-gather(f32[6,3072]{1,0:T(8,128)S(1)} %pad_maximum_fusion), channel_id=1, replica_groups=mesh['blk'=8,'grp'=32] {'blk'}, dimensions={1}, use_global_device_ids=true | all-gather | bytes 663552 | tf_op jit(solution)/shard_map/all_gather | solution.py:70
  117.7 128.9 %while.25 = (s32[]{:T(128)}, f32[3,1024]{1,0:T(4,128)S(1)}, f32[6,24576]{1,0:T(8,128)S(1)}, f32[3,1024]{1,0:T(4,128)S(1)}, f32[]{:T(128)}, /*index=5*/s32[]{:T(1...) while((s32[]{:T(128)}, f32[3,1024]{1,0:T(4,128)S(1)}, ...), condition=%wide.region_3.0_spmd.clone, body=%wide.region_2.0_spmd.clone.sunk | while | flops 54532104 | bytes 119025 | solution.py:45
  117.8 5.3 %fusion.61 = f32[3,1024]{1,0:T(4,128)S(1)} fusion(f32[]{:T(128)} %get-tuple-element.335, f32[1024]{0:T(1024)S(1)} %bitcast.45, f32[1024]{0:T(1024)S(1)} %bitcast.43, f32[1024]{0:T(1024)S(1)} %bitcast.44, f32[1024]{0:T(1024)S(1)} %bitcast.42, f32[1024]{0:T(1024)S(1)} %bitcast.46, f32[1024]{0:T(1024)S(1)} %bitcast.41, ...), kind=kOutput, calls=%fused_computation.19.clone.1 | convolution fusion | flops 54532096 | bytes 69645 | tf_op jit(solution)/shard_map/while/body/eval_jaxpr/dot_general | solution.py:41
  123.2 5.3 %fusion.61 = f32[3,1024]{1,0:T(4,128)S(1)} fusion(f32[]{:T(128)} %get-tuple-element.335, f32[1024]{0:T(1024)S(1)} %bitcast.45, f32[1024]{0:T(1024)S(1)} %bitcast.43, f32[1024]{0:T(1024)S(1)} %bitcast.44, f32[1024]{0:T(1024)S(1)} %bitcast.42, f32[1024]{0:T(1024)S(1)} %bitcast.46, f32[1024]{0:T(1024)S(1)} %bitcast.41, ...), kind=kOutput, calls=%fused_computation.19.clone.1 | convolution fusion | flops 54532096 | bytes 69645 | tf_op jit(solution)/shard_map/while/body/eval_jaxpr/dot_general | solution.py:41
  128.5 5.3 %fusion.61 = f32[3,1024]{1,0:T(4,128)S(1)} fusion(f32[]{:T(128)} %get-tuple-element.335, f32[1024]{0:T(1024)S(1)} %bitcast.45, f32[1024]{0:T(1024)S(1)} %bitcast.43, f32[1024]{0:T(1024)S(1)} %bitcast.44, f32[1024]{0:T(1024)S(1)} %bitcast.42, f32[1024]{0:T(1024)S(1)} %bitcast.46, f32[1024]{0:T(1024)S(1)} %bitcast.41, ...), kind=kOutput, calls=%fused_computation.19.clone.1 | convolution fusion | flops 54532096 | bytes 69645 | tf_op jit(solution)/shard_map/while/body/eval_jaxpr/dot_general | solution.py:41
  133.9 5.3 %fusion.61 = f32[3,1024]{1,0:T(4,128)S(1)} fusion(f32[]{:T(128)} %get-tuple-element.335, f32[1024]{0:T(1024)S(1)} %bitcast.45, f32[1024]{0:T(1024)S(1)} %bitcast.43, f32[1024]{0:T(1024)S(1)} %bitcast.44, f32[1024]{0:T(1024)S(1)} %bitcast.42, f32[1024]{0:T(1024)S(1)} %bitcast.46, f32[1024]{0:T(1024)S(1)} %bitcast.41, ...), kind=kOutput, calls=%fused_computation.19.clone.1 | convolution fusion | flops 54532096 | bytes 69645 | tf_op jit(solution)/shard_map/while/body/eval_jaxpr/dot_general | solution.py:41
  139.3 5.3 %fusion.61 = f32[3,1024]{1,0:T(4,128)S(1)} fusion(f32[]{:T(128)} %get-tuple-element.335, f32[1024]{0:T(1024)S(1)} %bitcast.45, f32[1024]{0:T(1024)S(1)} %bitcast.43, f32[1024]{0:T(1024)S(1)} %bitcast.44, f32[1024]{0:T(1024)S(1)} %bitcast.42, f32[1024]{0:T(1024)S(1)} %bitcast.46, f32[1024]{0:T(1024)S(1)} %bitcast.41, ...), kind=kOutput, calls=%fused_computation.19.clone.1 | convolution fusion | flops 54532096 | bytes 69645 | tf_op jit(solution)/shard_map/while/body/eval_jaxpr/dot_general | solution.py:41
  144.6 5.3 %fusion.61 = f32[3,1024]{1,0:T(4,128)S(1)} fusion(f32[]{:T(128)} %get-tuple-element.335, f32[1024]{0:T(1024)S(1)} %bitcast.45, f32[1024]{0:T(1024)S(1)} %bitcast.43, f32[1024]{0:T(1024)S(1)} %bitcast.44, f32[1024]{0:T(1024)S(1)} %bitcast.42, f32[1024]{0:T(1024)S(1)} %bitcast.46, f32[1024]{0:T(1024)S(1)} %bitcast.41, ...), kind=kOutput, calls=%fused_computation.19.clone.1 | convolution fusion | flops 54532096 | bytes 69645 | tf_op jit(solution)/shard_map/while/body/eval_jaxpr/dot_general | solution.py:41
  150.0 5.3 %fusion.61 = f32[3,1024]{1,0:T(4,128)S(1)} fusion(f32[]{:T(128)} %get-tuple-element.335, f32[1024]{0:T(1024)S(1)} %bitcast.45, f32[1024]{0:T(1024)S(1)} %bitcast.43, f32[1024]{0:T(1024)S(1)} %bitcast.44, f32[1024]{0:T(1024)S(1)} %bitcast.42, f32[1024]{0:T(1024)S(1)} %bitcast.46, f32[1024]{0:T(1024)S(1)} %bitcast.41, ...), kind=kOutput, calls=%fused_computation.19.clone.1 | convolution fusion | flops 54532096 | bytes 69645 | tf_op jit(solution)/shard_map/while/body/eval_jaxpr/dot_general | solution.py:41
  155.4 5.3 %fusion.61 = f32[3,1024]{1,0:T(4,128)S(1)} fusion(f32[]{:T(128)} %get-tuple-element.335, f32[1024]{0:T(1024)S(1)} %bitcast.45, f32[1024]{0:T(1024)S(1)} %bitcast.43, f32[1024]{0:T(1024)S(1)} %bitcast.44, f32[1024]{0:T(1024)S(1)} %bitcast.42, f32[1024]{0:T(1024)S(1)} %bitcast.46, f32[1024]{0:T(1024)S(1)} %bitcast.41, ...), kind=kOutput, calls=%fused_computation.19.clone.1 | convolution fusion | flops 54532096 | bytes 69645 | tf_op jit(solution)/shard_map/while/body/eval_jaxpr/dot_general | solution.py:41
  160.7 5.3 %fusion.61 = f32[3,1024]{1,0:T(4,128)S(1)} fusion(f32[]{:T(128)} %get-tuple-element.335, f32[1024]{0:T(1024)S(1)} %bitcast.45, f32[1024]{0:T(1024)S(1)} %bitcast.43, f32[1024]{0:T(1024)S(1)} %bitcast.44, f32[1024]{0:T(1024)S(1)} %bitcast.42, f32[1024]{0:T(1024)S(1)} %bitcast.46, f32[1024]{0:T(1024)S(1)} %bitcast.41, ...), kind=kOutput, calls=%fused_computation.19.clone.1 | convolution fusion | flops 54532096 | bytes 69645 | tf_op jit(solution)/shard_map/while/body/eval_jaxpr/dot_general | solution.py:41
  166.1 5.3 %fusion.61 = f32[3,1024]{1,0:T(4,128)S(1)} fusion(f32[]{:T(128)} %get-tuple-element.335, f32[1024]{0:T(1024)S(1)} %bitcast.45, f32[1024]{0:T(1024)S(1)} %bitcast.43, f32[1024]{0:T(1024)S(1)} %bitcast.44, f32[1024]{0:T(1024)S(1)} %bitcast.42, f32[1024]{0:T(1024)S(1)} %bitcast.46, f32[1024]{0:T(1024)S(1)} %bitcast.41, ...), kind=kOutput, calls=%fused_computation.19.clone.1 | convolution fusion | flops 54532096 | bytes 69645 | tf_op jit(solution)/shard_map/while/body/eval_jaxpr/dot_general | solution.py:41
  171.5 5.3 %fusion.61 = f32[3,1024]{1,0:T(4,128)S(1)} fusion(f32[]{:T(128)} %get-tuple-element.335, f32[1024]{0:T(1024)S(1)} %bitcast.45, f32[1024]{0:T(1024)S(1)} %bitcast.43, f32[1024]{0:T(1024)S(1)} %bitcast.44, f32[1024]{0:T(1024)S(1)} %bitcast.42, f32[1024]{0:T(1024)S(1)} %bitcast.46, f32[1024]{0:T(1024)S(1)} %bitcast.41, ...), kind=kOutput, calls=%fused_computation.19.clone.1 | convolution fusion | flops 54532096 | bytes 69645 | tf_op jit(solution)/shard_map/while/body/eval_jaxpr/dot_general | solution.py:41
  176.9 5.3 %fusion.61 = f32[3,1024]{1,0:T(4,128)S(1)} fusion(f32[]{:T(128)} %get-tuple-element.335, f32[1024]{0:T(1024)S(1)} %bitcast.45, f32[1024]{0:T(1024)S(1)} %bitcast.43, f32[1024]{0:T(1024)S(1)} %bitcast.44, f32[1024]{0:T(1024)S(1)} %bitcast.42, f32[1024]{0:T(1024)S(1)} %bitcast.46, f32[1024]{0:T(1024)S(1)} %bitcast.41, ...), kind=kOutput, calls=%fused_computation.19.clone.1 | convolution fusion | flops 54532096 | bytes 69645 | tf_op jit(solution)/shard_map/while/body/eval_jaxpr/dot_general | solution.py:41
  182.2 5.3 %fusion.61 = f32[3,1024]{1,0:T(4,128)S(1)} fusion(f32[]{:T(128)} %get-tuple-element.335, f32[1024]{0:T(1024)S(1)} %bitcast.45, f32[1024]{0:T(1024)S(1)} %bitcast.43, f32[1024]{0:T(1024)S(1)} %bitcast.44, f32[1024]{0:T(1024)S(1)} %bitcast.42, f32[1024]{0:T(1024)S(1)} %bitcast.46, f32[1024]{0:T(1024)S(1)} %bitcast.41, ...), kind=kOutput, calls=%fused_computation.19.clone.1 | convolution fusion | flops 54532096 | bytes 69645 | tf_op jit(solution)/shard_map/while/body/eval_jaxpr/dot_general | solution.py:41
  187.6 5.3 %fusion.61 = f32[3,1024]{1,0:T(4,128)S(1)} fusion(f32[]{:T(128)} %get-tuple-element.335, f32[1024]{0:T(1024)S(1)} %bitcast.45, f32[1024]{0:T(1024)S(1)} %bitcast.43, f32[1024]{0:T(1024)S(1)} %bitcast.44, f32[1024]{0:T(1024)S(1)} %bitcast.42, f32[1024]{0:T(1024)S(1)} %bitcast.46, f32[1024]{0:T(1024)S(1)} %bitcast.41, ...), kind=kOutput, calls=%fused_computation.19.clone.1 | convolution fusion | flops 54532096 | bytes 69645 | tf_op jit(solution)/shard_map/while/body/eval_jaxpr/dot_general | solution.py:41
  193.0 5.3 %fusion.61 = f32[3,1024]{1,0:T(4,128)S(1)} fusion(f32[]{:T(128)} %get-tuple-element.335, f32[1024]{0:T(1024)S(1)} %bitcast.45, f32[1024]{0:T(1024)S(1)} %bitcast.43, f32[1024]{0:T(1024)S(1)} %bitcast.44, f32[1024]{0:T(1024)S(1)} %bitcast.42, f32[1024]{0:T(1024)S(1)} %bitcast.46, f32[1024]{0:T(1024)S(1)} %bitcast.41, ...), kind=kOutput, calls=%fused_computation.19.clone.1 | convolution fusion | flops 54532096 | bytes 69645 | tf_op jit(solution)/shard_map/while/body/eval_jaxpr/dot_general | solution.py:41
  198.3 5.3 %fusion.61 = f32[3,1024]{1,0:T(4,128)S(1)} fusion(f32[]{:T(128)} %get-tuple-element.335, f32[1024]{0:T(1024)S(1)} %bitcast.45, f32[1024]{0:T(1024)S(1)} %bitcast.43, f32[1024]{0:T(1024)S(1)} %bitcast.44, f32[1024]{0:T(1024)S(1)} %bitcast.42, f32[1024]{0:T(1024)S(1)} %bitcast.46, f32[1024]{0:T(1024)S(1)} %bitcast.41, ...), kind=kOutput, calls=%fused_computation.19.clone.1 | convolution fusion | flops 54532096 | bytes 69645 | tf_op jit(solution)/shard_map/while/body/eval_jaxpr/dot_general | solution.py:41
  203.7 5.3 %fusion.61 = f32[3,1024]{1,0:T(4,128)S(1)} fusion(f32[]{:T(128)} %get-tuple-element.335, f32[1024]{0:T(1024)S(1)} %bitcast.45, f32[1024]{0:T(1024)S(1)} %bitcast.43, f32[1024]{0:T(1024)S(1)} %bitcast.44, f32[1024]{0:T(1024)S(1)} %bitcast.42, f32[1024]{0:T(1024)S(1)} %bitcast.46, f32[1024]{0:T(1024)S(1)} %bitcast.41, ...), kind=kOutput, calls=%fused_computation.19.clone.1 | convolution fusion | flops 54532096 | bytes 69645 | tf_op jit(solution)/shard_map/while/body/eval_jaxpr/dot_general | solution.py:41
  209.1 5.3 %fusion.61 = f32[3,1024]{1,0:T(4,128)S(1)} fusion(f32[]{:T(128)} %get-tuple-element.335, f32[1024]{0:T(1024)S(1)} %bitcast.45, f32[1024]{0:T(1024)S(1)} %bitcast.43, f32[1024]{0:T(1024)S(1)} %bitcast.44, f32[1024]{0:T(1024)S(1)} %bitcast.42, f32[1024]{0:T(1024)S(1)} %bitcast.46, f32[1024]{0:T(1024)S(1)} %bitcast.41, ...), kind=kOutput, calls=%fused_computation.19.clone.1 | convolution fusion | flops 54532096 | bytes 69645 | tf_op jit(solution)/shard_map/while/body/eval_jaxpr/dot_general | solution.py:41
  214.5 5.3 %fusion.61 = f32[3,1024]{1,0:T(4,128)S(1)} fusion(f32[]{:T(128)} %get-tuple-element.335, f32[1024]{0:T(1024)S(1)} %bitcast.45, f32[1024]{0:T(1024)S(1)} %bitcast.43, f32[1024]{0:T(1024)S(1)} %bitcast.44, f32[1024]{0:T(1024)S(1)} %bitcast.42, f32[1024]{0:T(1024)S(1)} %bitcast.46, f32[1024]{0:T(1024)S(1)} %bitcast.41, ...), kind=kOutput, calls=%fused_computation.19.clone.1 | convolution fusion | flops 54532096 | bytes 69645 | tf_op jit(solution)/shard_map/while/body/eval_jaxpr/dot_general | solution.py:41
  219.8 5.3 %fusion.61 = f32[3,1024]{1,0:T(4,128)S(1)} fusion(f32[]{:T(128)} %get-tuple-element.335, f32[1024]{0:T(1024)S(1)} %bitcast.45, f32[1024]{0:T(1024)S(1)} %bitcast.43, f32[1024]{0:T(1024)S(1)} %bitcast.44, f32[1024]{0:T(1024)S(1)} %bitcast.42, f32[1024]{0:T(1024)S(1)} %bitcast.46, f32[1024]{0:T(1024)S(1)} %bitcast.41, ...), kind=kOutput, calls=%fused_computation.19.clone.1 | convolution fusion | flops 54532096 | bytes 69645 | tf_op jit(solution)/shard_map/while/body/eval_jaxpr/dot_general | solution.py:41
  225.2 5.3 %fusion.61 = f32[3,1024]{1,0:T(4,128)S(1)} fusion(f32[]{:T(128)} %get-tuple-element.335, f32[1024]{0:T(1024)S(1)} %bitcast.45, f32[1024]{0:T(1024)S(1)} %bitcast.43, f32[1024]{0:T(1024)S(1)} %bitcast.44, f32[1024]{0:T(1024)S(1)} %bitcast.42, f32[1024]{0:T(1024)S(1)} %bitcast.46, f32[1024]{0:T(1024)S(1)} %bitcast.41, ...), kind=kOutput, calls=%fused_computation.19.clone.1 | convolution fusion | flops 54532096 | bytes 69645 | tf_op jit(solution)/shard_map/while/body/eval_jaxpr/dot_general | solution.py:41
  230.6 5.3 %fusion.61 = f32[3,1024]{1,0:T(4,128)S(1)} fusion(f32[]{:T(128)} %get-tuple-element.335, f32[1024]{0:T(1024)S(1)} %bitcast.45, f32[1024]{0:T(1024)S(1)} %bitcast.43, f32[1024]{0:T(1024)S(1)} %bitcast.44, f32[1024]{0:T(1024)S(1)} %bitcast.42, f32[1024]{0:T(1024)S(1)} %bitcast.46, f32[1024]{0:T(1024)S(1)} %bitcast.41, ...), kind=kOutput, calls=%fused_computation.19.clone.1 | convolution fusion | flops 54532096 | bytes 69645 | tf_op jit(solution)/shard_map/while/body/eval_jaxpr/dot_general | solution.py:41
  235.9 5.3 %fusion.61 = f32[3,1024]{1,0:T(4,128)S(1)} fusion(f32[]{:T(128)} %get-tuple-element.335, f32[1024]{0:T(1024)S(1)} %bitcast.45, f32[1024]{0:T(1024)S(1)} %bitcast.43, f32[1024]{0:T(1024)S(1)} %bitcast.44, f32[1024]{0:T(1024)S(1)} %bitcast.42, f32[1024]{0:T(1024)S(1)} %bitcast.46, f32[1024]{0:T(1024)S(1)} %bitcast.41, ...), kind=kOutput, calls=%fused_computation.19.clone.1 | convolution fusion | flops 54532096 | bytes 69645 | tf_op jit(solution)/shard_map/while/body/eval_jaxpr/dot_general | solution.py:41
  241.3 5.3 %fusion.61 = f32[3,1024]{1,0:T(4,128)S(1)} fusion(f32[]{:T(128)} %get-tuple-element.335, f32[1024]{0:T(1024)S(1)} %bitcast.45, f32[1024]{0:T(1024)S(1)} %bitcast.43, f32[1024]{0:T(1024)S(1)} %bitcast.44, f32[1024]{0:T(1024)S(1)} %bitcast.42, f32[1024]{0:T(1024)S(1)} %bitcast.46, f32[1024]{0:T(1024)S(1)} %bitcast.41, ...), kind=kOutput, calls=%fused_computation.19.clone.1 | convolution fusion | flops 54532096 | bytes 69645 | tf_op jit(solution)/shard_map/while/body/eval_jaxpr/dot_general | solution.py:41
  246.7 82.2 %psum.22 = f32[3]{0:T(128)S(1)} all-reduce(f32[3]{0:T(128)S(1)} %multiply_reduce_fusion), channel_id=1, replica_groups=mesh['blk'=8,'grp'=32] {'blk','grp'}, use_global_device_ids=true, to_apply=%region_5.0 | all-reduce | flops 3 | bytes 24 | tf_op jit(solution)/shard_map/psum | solution.py:76
  329.0 0.8 fusion.50
  329.8 74.3 %psum.23 = f32[3]{0:T(128)} all-reduce(f32[3]{0:T(128)S(1)} %get-tuple-element.194), channel_id=1, replica_groups=mesh['blk'=8,'grp'=32] {'blk','grp'}, use_global_device_ids=true, to_apply=%region_7.0 | all-reduce | flops 3 | bytes 24 | tf_op jit(solution)/shard_map/psum | solution.py:80
  404.1 42.1 %all_gather.7 = f32[6,32768]{1,0:T(8,128)S(1)} all-gather(f32[6,1024]{1,0:T(8,128)S(1)} %pad_maximum_fusion.1), channel_id=1, replica_groups=mesh['blk'=8,'grp'=32] {'grp'}, dimensions={1}, use_global_device_ids=true | all-gather | bytes 811008 | tf_op jit(solution)/shard_map/all_gather | solution.py:91
  446.2 27.0 %while.26 = (s32[]{:T(128)}, f32[3,1024]{1,0:T(4,128)S(1)}, s32[4]{0:T(128)S(1)}, f32[6,32768]{1,0:T(8,128)S(1)}, f32[3,1024]{1,0:T(4,128)S(1)}, /*index=5*/f32[...) while((s32[]{:T(128)}, f32[3,1024]{1,0:T(4,128)S(1)}, ...), condition=%wide.region_9.10_spmd.clone, body=%wide.region_8.9_spmd.clone.sunk | while | flops 54532104 | bytes 119045 | solution.py:97
  446.2 0.7 dynamic_slice.18
  447.7 5.3 %fusion.64 = f32[3,1024]{1,0:T(4,128)S(1)} fusion(f32[]{:T(128)} %get-tuple-element.374, f32[1024]{0:T(1024)S(1)} %bitcast.51, f32[1024]{0:T(1024)S(1)} %bitcast.49, f32[1024]{0:T(1024)S(1)} %bitcast.50, f32[1024]{0:T(1024)S(1)} %bitcast.48, f32[1024]{0:T(1024)S(1)} %bitcast.52, f32[1024]{0:T(1024)S(1)} %bitcast.47, ...), kind=kOutput, calls=%fused_computation.44.clone.1 | convolution fusion | flops 54532096 | bytes 69645 | tf_op jit(solution)/shard_map/while/body/eval_jaxpr/dot_general | solution.py:87
  453.0 0.7 dynamic_slice.18
  454.4 5.3 %fusion.64 = f32[3,1024]{1,0:T(4,128)S(1)} fusion(f32[]{:T(128)} %get-tuple-element.374, f32[1024]{0:T(1024)S(1)} %bitcast.51, f32[1024]{0:T(1024)S(1)} %bitcast.49, f32[1024]{0:T(1024)S(1)} %bitcast.50, f32[1024]{0:T(1024)S(1)} %bitcast.48, f32[1024]{0:T(1024)S(1)} %bitcast.52, f32[1024]{0:T(1024)S(1)} %bitcast.47, ...), kind=kOutput, calls=%fused_computation.44.clone.1 | convolution fusion | flops 54532096 | bytes 69645 | tf_op jit(solution)/shard_map/while/body/eval_jaxpr/dot_general | solution.py:87
  459.7 0.7 dynamic_slice.18
  461.2 5.3 %fusion.64 = f32[3,1024]{1,0:T(4,128)S(1)} fusion(f32[]{:T(128)} %get-tuple-element.374, f32[1024]{0:T(1024)S(1)} %bitcast.51, f32[1024]{0:T(1024)S(1)} %bitcast.49, f32[1024]{0:T(1024)S(1)} %bitcast.50, f32[1024]{0:T(1024)S(1)} %bitcast.48, f32[1024]{0:T(1024)S(1)} %bitcast.52, f32[1024]{0:T(1024)S(1)} %bitcast.47, ...), kind=kOutput, calls=%fused_computation.44.clone.1 | convolution fusion | flops 54532096 | bytes 69645 | tf_op jit(solution)/shard_map/while/body/eval_jaxpr/dot_general | solution.py:87
  466.5 0.7 dynamic_slice.18
  467.9 5.3 %fusion.64 = f32[3,1024]{1,0:T(4,128)S(1)} fusion(f32[]{:T(128)} %get-tuple-element.374, f32[1024]{0:T(1024)S(1)} %bitcast.51, f32[1024]{0:T(1024)S(1)} %bitcast.49, f32[1024]{0:T(1024)S(1)} %bitcast.50, f32[1024]{0:T(1024)S(1)} %bitcast.48, f32[1024]{0:T(1024)S(1)} %bitcast.52, f32[1024]{0:T(1024)S(1)} %bitcast.47, ...), kind=kOutput, calls=%fused_computation.44.clone.1 | convolution fusion | flops 54532096 | bytes 69645 | tf_op jit(solution)/shard_map/while/body/eval_jaxpr/dot_general | solution.py:87
  (53 shorter events, 3.8 us)
Async XLA Ops:
  0.6 117.0 %copy-start = (f32[3,1024]{1,0:T(4,128)S(1)}, f32[3,1024]{1,0:T(4,128)}, u32[]{:S(2)}) copy-start(f32[3,1024]{1,0:T(4,128)} %param.13) | copy-start | bytes 36868
  85.0 243.9 %copy-start.1 = (f32[3,1024]{1,0:T(4,128)}, f32[3,1024]{1,0:T(4,128)S(1)}, u32[]{:S(2)}) copy-start(f32[3,1024]{1,0:T(4,128)S(1)} %multiply_add_fusion.2) | copy-start | bytes 36868
  85.8 6.2 %collective-permute-start.1 = (f32[6,1024]{1,0:T(8,128)S(1)}, f32[6,1024]{1,0:T(8,128)S(1)}, u32[]{:S(2)}, u32[]{:S(2)}) collective-permute-start(f32[6,1024]{1,0:T(8,128)S(1)} %pad_maximum_fusion.2), channel_id=1, source_target_pairs={{1,0},{2,1},{3,2},{4,3},{5,4},{6,5},{7,6},{8,7},{9,8},{10,9},{11,1... | collective-permute-start | bytes 73736 | tf_op jit(solution)/shard_map/ppermute | solution.py:17
  88.7 3.7 collective-permute-start
  117.7 128.9 %copy-start.5 = (f32[1024]{0:T(1024)S(1)}, f32[1024]{0:T(1024)}, u32[]{:S(2)}) copy-start(f32[1024]{0:T(1024)} %param.17) | copy-start | bytes 12292
  117.7 211.3 %copy-start.3 = (f32[3,1024]{1,0:T(4,128)S(1)}, f32[3,1024]{1,0:T(4,128)}, u32[]{:S(2)}) copy-start(f32[3,1024]{1,0:T(4,128)} %param.15) | copy-start | bytes 36868
  117.7 211.3 %copy-start.6 = (f32[3,1024]{1,0:T(4,128)S(1)}, f32[3,1024]{1,0:T(4,128)}, u32[]{:S(2)}) copy-start(f32[3,1024]{1,0:T(4,128)} %param.14) | copy-start | bytes 36868
  246.6 199.6 %copy-start.2 = (f32[3,1024]{1,0:T(4,128)S(1)}, f32[3,1024]{1,0:T(4,128)}, u32[]{:S(2)}) copy-start(f32[3,1024]{1,0:T(4,128)} %param.20) | copy-start | bytes 36868
  246.6 199.6 %copy-start.7 = (s32[1,4]{1,0:T(1,128)S(1)}, s32[1,4]{1,0:T(1,128)}, u32[]{:S(2)}) copy-start(s32[1,4]{1,0:T(1,128)} %param.21) | copy-start | bytes 52
  329.8 116.5 %copy-start.4 = (f32[3,1024]{1,0:T(4,128)}, f32[3,1024]{1,0:T(4,128)S(1)}, u32[]{:S(2)}) copy-start(f32[3,1024]{1,0:T(4,128)S(1)} %get-tuple-element.214) | copy-start | bytes 36868
  473.2 0.6 copy-start.8
where the time goes:
time: 475 us; the launch traced here: 474 us
  blocking collectives  305 us (64%)
  matrix products  148 us (31%)
  local copies, waits for them, and re-layouts  5.95 us (1%)
  starting transfers between devices  5.56 us (1%)
  other arithmetic  5.41 us (1%)
    dot_general x24, matrix products, one(): jnp.dot(block[3:], weights, preferred_element_type=jnp.float32, precision...  127 us
    psum x1, blocking collectives, per_device(): curvature = lax.psum(jnp.sum(direction * image, axis=1), ('blk', 'grp'))  82.2 us
    psum x1, blocking collectives, per_device(): norm_now = lax.psum(jnp.sum(residual * precond, axis=1), ('blk', 'grp'))  81.4 us
    psum x1, blocking collectives, per_device(): lax.psum(jnp.sum(residual_next * residual_next / scaling, axis=1), ('blk'...  74.3 us
    all_gather x1, blocking collectives, per_device(): sector_bands = lax.all_gather(stacked, 'grp', axis=1, tiled=True)  42.1 us
    all_gather x1, blocking collectives, per_device(): lax.all_gather(widened, 'blk', axis=1, tiled=True)  24.6 us
    dot_general x4, matrix products, contribution(): jnp.dot(block[3:], weights, preferred_element_type=jnp.float32, precision...  21.1 us
  transfers between devices with their start and end apart: 2, of which 1 were waited for; matrix products, arithmetic and copies ran while one was open for 0% of the time, Pallas kernels for 0%

commit v1 on v0

--- a/solution.py
+++ b/solution.py
@@ -67,7 +67,12 @@
     widened = extended(bundle, (("grp", 1),), count)
     kernel_part = apply_blocks(
         jnp.zeros((3, count), jnp.float32),
-        lax.all_gather(widened, "blk", axis=1, tiled=True),
+        jnp.concatenate(
+            lax.all_to_all(
+                jnp.stack(lax.psum(1, "blk") * [widened]), "blk", split_axis=0, concat_axis=0
+            ),
+            axis=1,
+        ),
         centres,
         count,
         radius,

time: 475 us -> 459 us (0.966)
  blocking collectives: 305 us -> 273 us
  waiting for transfers between devices: 0.34 us -> 13.5 us
    all_gather x1 -> x0, blocking collectives: 24.6 us -> none  [per_device(): lax.all_gather(widened, 'blk', axis=1, tiled=True)]
    all_to_all x0 -> x1, waiting for transfers between devices: none -> 10.2 us  [per_device(): lax.all_to_all(jnp.stack(lax.psum(1, 'blk') * [widened]), 'blk', split_ax...]
    psum x1, blocking collectives: 82.2 us -> 75.9 us  [per_device(): curvature = lax.psum(jnp.sum(direction * image, axis=1), ('blk', 'grp'))]
  transfers between devices with their start and end apart: 2 -> 3, of which waited for: 1 -> 2; matrix products, arithmetic and copies ran while one was open for 0% -> 0% of each run, Pallas kernels for 0% -> 0%
where the time goes in v1:
time: 459 us; the launch traced here: 458 us
  blocking collectives  273 us (59%)
  matrix products  148 us (32%)
  waiting for transfers between devices  13.5 us (3%)
  starting transfers between devices  8.78 us (2%)
  local copies, waits for them, and re-layouts  5.93 us (1%)
  other arithmetic  5.41 us (1%)
    dot_general x24, matrix products, one(): jnp.dot(block[3:], weights, preferred_element_type=jnp.float32, precision...  127 us
    psum x1, blocking collectives, per_device(): norm_now = lax.psum(jnp.sum(residual * precond, axis=1), ('blk', 'grp'))  81.4 us
    psum x1, blocking collectives, per_device(): curvature = lax.psum(jnp.sum(direction * image, axis=1), ('blk', 'grp'))  75.9 us
    psum x1, blocking collectives, per_device(): lax.psum(jnp.sum(residual_next * residual_next / scaling, axis=1), ('blk'...  73.3 us
    all_gather x1, blocking collectives, per_device(): sector_bands = lax.all_gather(stacked, 'grp', axis=1, tiled=True)  42.5 us
    dot_general x4, matrix products, contribution(): jnp.dot(block[3:], weights, preferred_element_type=jnp.float32, precision...  21.1 us
    all_to_all x1, waiting for transfers between devices, per_device(): lax.all_to_all(jnp.stack(lax.psum(1, 'blk') * [widened]), 'blk', split_ax...  10.2 us
  transfers between devices with their start and end apart: 3, of which 2 were waited for; matrix products, arithmetic and copies ran while one was open for 0% of the time, Pallas kernels for 0%

profile of v1, /device:TPU:1, one launch (start us, length us, event | category | flops | bytes accessed | tf_op | source)
XLA Modules:
  0.0 458.2 jit_solution(6705032458852215001)
XLA Ops:
  0.6 0.7 broadcast_add_fusion
  1.3 0.8 multiply_reduce_fusion.1
  2.2 81.4 %psum.21 = f32[3]{0:T(128)S(1)} all-reduce(f32[3]{0:T(128)S(1)} %multiply_reduce_fusion.1), channel_id=1, replica_groups=mesh['blk'=8,'grp'=32] {'blk','grp'}, use_global_device_ids=true, to_apply=%region_1.0 | all-reduce | flops 3 | bytes 24 | tf_op jit(solution)/shard_map/psum | solution.py:63
  83.6 0.7 div.42
  84.2 0.8 multiply_add_fusion.2
  85.0 0.7 pad_maximum_fusion.2
  85.8 3.3 collective-permute-start
  89.1 1.9 collective-permute-start.1
  91.0 3.3 collective-permute-done.1
  94.3 0.7 pad_maximum_fusion
  95.1 0.9 stack.2
  96.0 3.5 all-to-all-start
  100.2 10.2 %all-to-all-done = f32[8,6,3072]{2,1,0:T(8,128)S(1)} async-done(((f32[8,6,3072]{2,1,0:T(8,128)}), f32[8,6,3072]{2,1,0:T(8,128)S(1)}, u32[]{:S(2)}, u32[]{:S(2)}) %all-to-all-start) | async-done | bytes 589856 | tf_op jit(solution)/shard_map/all_to_all | solution.py:71
  110.5 128.9 %while.25 = (s32[]{:T(128)}, f32[3,1024]{1,0:T(4,128)S(1)}, f32[6,24576]{1,0:T(8,128)S(1)}, f32[3,1024]{1,0:T(4,128)S(1)}, f32[]{:T(128)}, /*index=5*/s32[]{:T(1...) while((s32[]{:T(128)}, f32[3,1024]{1,0:T(4,128)S(1)}, ...), condition=%wide.region_3.0_spmd.clone, body=%wide.region_2.0_spmd.clone.sunk | while | flops 54532104 | bytes 119017 | solution.py:45
  110.6 5.3 %fusion.61 = f32[3,1024]{1,0:T(4,128)S(1)} fusion(f32[]{:T(128)} %get-tuple-element.335, f32[1024]{0:T(1024)S(1)} %bitcast.49, f32[1024]{0:T(1024)S(1)} %bitcast.47, f32[1024]{0:T(1024)S(1)} %bitcast.48, f32[1024]{0:T(1024)S(1)} %bitcast.46, f32[1024]{0:T(1024)S(1)} %bitcast.50, f32[1024]{0:T(1024)S(1)} %bitcast.45, ...), kind=kOutput, calls=%fused_computation.19.clone.1 | convolution fusion | flops 54532096 | bytes 69645 | tf_op jit(solution)/shard_map/while/body/eval_jaxpr/dot_general | solution.py:41
  116.0 5.3 %fusion.61 = f32[3,1024]{1,0:T(4,128)S(1)} fusion(f32[]{:T(128)} %get-tuple-element.335, f32[1024]{0:T(1024)S(1)} %bitcast.49, f32[1024]{0:T(1024)S(1)} %bitcast.47, f32[1024]{0:T(1024)S(1)} %bitcast.48, f32[1024]{0:T(1024)S(1)} %bitcast.46, f32[1024]{0:T(1024)S(1)} %bitcast.50, f32[1024]{0:T(1024)S(1)} %bitcast.45, ...), kind=kOutput, calls=%fused_computation.19.clone.1 | convolution fusion | flops 54532096 | bytes 69645 | tf_op jit(solution)/shard_map/while/body/eval_jaxpr/dot_general | solution.py:41
  121.3 5.3 %fusion.61 = f32[3,1024]{1,0:T(4,128)S(1)} fusion(f32[]{:T(128)} %get-tuple-element.335, f32[1024]{0:T(1024)S(1)} %bitcast.49, f32[1024]{0:T(1024)S(1)} %bitcast.47, f32[1024]{0:T(1024)S(1)} %bitcast.48, f32[1024]{0:T(1024)S(1)} %bitcast.46, f32[1024]{0:T(1024)S(1)} %bitcast.50, f32[1024]{0:T(1024)S(1)} %bitcast.45, ...), kind=kOutput, calls=%fused_computation.19.clone.1 | convolution fusion | flops 54532096 | bytes 69645 | tf_op jit(solution)/shard_map/while/body/eval_jaxpr/dot_general | solution.py:41
  126.7 5.3 %fusion.61 = f32[3,1024]{1,0:T(4,128)S(1)} fusion(f32[]{:T(128)} %get-tuple-element.335, f32[1024]{0:T(1024)S(1)} %bitcast.49, f32[1024]{0:T(1024)S(1)} %bitcast.47, f32[1024]{0:T(1024)S(1)} %bitcast.48, f32[1024]{0:T(1024)S(1)} %bitcast.46, f32[1024]{0:T(1024)S(1)} %bitcast.50, f32[1024]{0:T(1024)S(1)} %bitcast.45, ...), kind=kOutput, calls=%fused_computation.19.clone.1 | convolution fusion | flops 54532096 | bytes 69645 | tf_op jit(solution)/shard_map/while/body/eval_jaxpr/dot_general | solution.py:41
  132.1 5.3 %fusion.61 = f32[3,1024]{1,0:T(4,128)S(1)} fusion(f32[]{:T(128)} %get-tuple-element.335, f32[1024]{0:T(1024)S(1)} %bitcast.49, f32[1024]{0:T(1024)S(1)} %bitcast.47, f32[1024]{0:T(1024)S(1)} %bitcast.48, f32[1024]{0:T(1024)S(1)} %bitcast.46, f32[1024]{0:T(1024)S(1)} %bitcast.50, f32[1024]{0:T(1024)S(1)} %bitcast.45, ...), kind=kOutput, calls=%fused_computation.19.clone.1 | convolution fusion | flops 54532096 | bytes 69645 | tf_op jit(solution)/shard_map/while/body/eval_jaxpr/dot_general | solution.py:41
  137.4 5.3 %fusion.61 = f32[3,1024]{1,0:T(4,128)S(1)} fusion(f32[]{:T(128)} %get-tuple-element.335, f32[1024]{0:T(1024)S(1)} %bitcast.49, f32[1024]{0:T(1024)S(1)} %bitcast.47, f32[1024]{0:T(1024)S(1)} %bitcast.48, f32[1024]{0:T(1024)S(1)} %bitcast.46, f32[1024]{0:T(1024)S(1)} %bitcast.50, f32[1024]{0:T(1024)S(1)} %bitcast.45, ...), kind=kOutput, calls=%fused_computation.19.clone.1 | convolution fusion | flops 54532096 | bytes 69645 | tf_op jit(solution)/shard_map/while/body/eval_jaxpr/dot_general | solution.py:41
  142.8 5.3 %fusion.61 = f32[3,1024]{1,0:T(4,128)S(1)} fusion(f32[]{:T(128)} %get-tuple-element.335, f32[1024]{0:T(1024)S(1)} %bitcast.49, f32[1024]{0:T(1024)S(1)} %bitcast.47, f32[1024]{0:T(1024)S(1)} %bitcast.48, f32[1024]{0:T(1024)S(1)} %bitcast.46, f32[1024]{0:T(1024)S(1)} %bitcast.50, f32[1024]{0:T(1024)S(1)} %bitcast.45, ...), kind=kOutput, calls=%fused_computation.19.clone.1 | convolution fusion | flops 54532096 | bytes 69645 | tf_op jit(solution)/shard_map/while/body/eval_jaxpr/dot_general | solution.py:41
  148.2 5.3 %fusion.61 = f32[3,1024]{1,0:T(4,128)S(1)} fusion(f32[]{:T(128)} %get-tuple-element.335, f32[1024]{0:T(1024)S(1)} %bitcast.49, f32[1024]{0:T(1024)S(1)} %bitcast.47, f32[1024]{0:T(1024)S(1)} %bitcast.48, f32[1024]{0:T(1024)S(1)} %bitcast.46, f32[1024]{0:T(1024)S(1)} %bitcast.50, f32[1024]{0:T(1024)S(1)} %bitcast.45, ...), kind=kOutput, calls=%fused_computation.19.clone.1 | convolution fusion | flops 54532096 | bytes 69645 | tf_op jit(solution)/shard_map/while/body/eval_jaxpr/dot_general | solution.py:41
  153.5 5.3 %fusion.61 = f32[3,1024]{1,0:T(4,128)S(1)} fusion(f32[]{:T(128)} %get-tuple-element.335, f32[1024]{0:T(1024)S(1)} %bitcast.49, f32[1024]{0:T(1024)S(1)} %bitcast.47, f32[1024]{0:T(1024)S(1)} %bitcast.48, f32[1024]{0:T(1024)S(1)} %bitcast.46, f32[1024]{0:T(1024)S(1)} %bitcast.50, f32[1024]{0:T(1024)S(1)} %bitcast.45, ...), kind=kOutput, calls=%fused_computation.19.clone.1 | convolution fusion | flops 54532096 | bytes 69645 | tf_op jit(solution)/shard_map/while/body/eval_jaxpr/dot_general | solution.py:41
  158.9 5.3 %fusion.61 = f32[3,1024]{1,0:T(4,128)S(1)} fusion(f32[]{:T(128)} %get-tuple-element.335, f32[1024]{0:T(1024)S(1)} %bitcast.49, f32[1024]{0:T(1024)S(1)} %bitcast.47, f32[1024]{0:T(1024)S(1)} %bitcast.48, f32[1024]{0:T(1024)S(1)} %bitcast.46, f32[1024]{0:T(1024)S(1)} %bitcast.50, f32[1024]{0:T(1024)S(1)} %bitcast.45, ...), kind=kOutput, calls=%fused_computation.19.clone.1 | convolution fusion | flops 54532096 | bytes 69645 | tf_op jit(solution)/shard_map/while/body/eval_jaxpr/dot_general | solution.py:41
  164.3 5.3 %fusion.61 = f32[3,1024]{1,0:T(4,128)S(1)} fusion(f32[]{:T(128)} %get-tuple-element.335, f32[1024]{0:T(1024)S(1)} %bitcast.49, f32[1024]{0:T(1024)S(1)} %bitcast.47, f32[1024]{0:T(1024)S(1)} %bitcast.48, f32[1024]{0:T(1024)S(1)} %bitcast.46, f32[1024]{0:T(1024)S(1)} %bitcast.50, f32[1024]{0:T(1024)S(1)} %bitcast.45, ...), kind=kOutput, calls=%fused_computation.19.clone.1 | convolution fusion | flops 54532096 | bytes 69645 | tf_op jit(solution)/shard_map/while/body/eval_jaxpr/dot_general | solution.py:41
  169.7 5.3 %fusion.61 = f32[3,1024]{1,0:T(4,128)S(1)} fusion(f32[]{:T(128)} %get-tuple-element.335, f32[1024]{0:T(1024)S(1)} %bitcast.49, f32[1024]{0:T(1024)S(1)} %bitcast.47, f32[1024]{0:T(1024)S(1)} %bitcast.48, f32[1024]{0:T(1024)S(1)} %bitcast.46, f32[1024]{0:T(1024)S(1)} %bitcast.50, f32[1024]{0:T(1024)S(1)} %bitcast.45, ...), kind=kOutput, calls=%fused_computation.19.clone.1 | convolution fusion | flops 54532096 | bytes 69645 | tf_op jit(solution)/shard_map/while/body/eval_jaxpr/dot_general | solution.py:41
  175.0 5.3 %fusion.61 = f32[3,1024]{1,0:T(4,128)S(1)} fusion(f32[]{:T(128)} %get-tuple-element.335, f32[1024]{0:T(1024)S(1)} %bitcast.49, f32[1024]{0:T(1024)S(1)} %bitcast.47, f32[1024]{0:T(1024)S(1)} %bitcast.48, f32[1024]{0:T(1024)S(1)} %bitcast.46, f32[1024]{0:T(1024)S(1)} %bitcast.50, f32[1024]{0:T(1024)S(1)} %bitcast.45, ...), kind=kOutput, calls=%fused_computation.19.clone.1 | convolution fusion | flops 54532096 | bytes 69645 | tf_op jit(solution)/shard_map/while/body/eval_jaxpr/dot_general | solution.py:41
  180.4 5.3 %fusion.61 = f32[3,1024]{1,0:T(4,128)S(1)} fusion(f32[]{:T(128)} %get-tuple-element.335, f32[1024]{0:T(1024)S(1)} %bitcast.49, f32[1024]{0:T(1024)S(1)} %bitcast.47, f32[1024]{0:T(1024)S(1)} %bitcast.48, f32[1024]{0:T(1024)S(1)} %bitcast.46, f32[1024]{0:T(1024)S(1)} %bitcast.50, f32[1024]{0:T(1024)S(1)} %bitcast.45, ...), kind=kOutput, calls=%fused_computation.19.clone.1 | convolution fusion | flops 54532096 | bytes 69645 | tf_op jit(solution)/shard_map/while/body/eval_jaxpr/dot_general | solution.py:41
  185.8 5.3 %fusion.61 = f32[3,1024]{1,0:T(4,128)S(1)} fusion(f32[]{:T(128)} %get-tuple-element.335, f32[1024]{0:T(1024)S(1)} %bitcast.49, f32[1024]{0:T(1024)S(1)} %bitcast.47, f32[1024]{0:T(1024)S(1)} %bitcast.48, f32[1024]{0:T(1024)S(1)} %bitcast.46, f32[1024]{0:T(1024)S(1)} %bitcast.50, f32[1024]{0:T(1024)S(1)} %bitcast.45, ...), kind=kOutput, calls=%fused_computation.19.clone.1 | convolution fusion | flops 54532096 | bytes 69645 | tf_op jit(solution)/shard_map/while/body/eval_jaxpr/dot_general | solution.py:41
  191.1 5.3 %fusion.61 = f32[3,1024]{1,0:T(4,128)S(1)} fusion(f32[]{:T(128)} %get-tuple-element.335, f32[1024]{0:T(1024)S(1)} %bitcast.49, f32[1024]{0:T(1024)S(1)} %bitcast.47, f32[1024]{0:T(1024)S(1)} %bitcast.48, f32[1024]{0:T(1024)S(1)} %bitcast.46, f32[1024]{0:T(1024)S(1)} %bitcast.50, f32[1024]{0:T(1024)S(1)} %bitcast.45, ...), kind=kOutput, calls=%fused_computation.19.clone.1 | convolution fusion | flops 54532096 | bytes 69645 | tf_op jit(solution)/shard_map/while/body/eval_jaxpr/dot_general | solution.py:41
  196.5 5.3 %fusion.61 = f32[3,1024]{1,0:T(4,128)S(1)} fusion(f32[]{:T(128)} %get-tuple-element.335, f32[1024]{0:T(1024)S(1)} %bitcast.49, f32[1024]{0:T(1024)S(1)} %bitcast.47, f32[1024]{0:T(1024)S(1)} %bitcast.48, f32[1024]{0:T(1024)S(1)} %bitcast.46, f32[1024]{0:T(1024)S(1)} %bitcast.50, f32[1024]{0:T(1024)S(1)} %bitcast.45, ...), kind=kOutput, calls=%fused_computation.19.clone.1 | convolution fusion | flops 54532096 | bytes 69645 | tf_op jit(solution)/shard_map/while/body/eval_jaxpr/dot_general | solution.py:41
  201.9 5.3 %fusion.61 = f32[3,1024]{1,0:T(4,128)S(1)} fusion(f32[]{:T(128)} %get-tuple-element.335, f32[1024]{0:T(1024)S(1)} %bitcast.49, f32[1024]{0:T(1024)S(1)} %bitcast.47, f32[1024]{0:T(1024)S(1)} %bitcast.48, f32[1024]{0:T(1024)S(1)} %bitcast.46, f32[1024]{0:T(1024)S(1)} %bitcast.50, f32[1024]{0:T(1024)S(1)} %bitcast.45, ...), kind=kOutput, calls=%fused_computation.19.clone.1 | convolution fusion | flops 54532096 | bytes 69645 | tf_op jit(solution)/shard_map/while/body/eval_jaxpr/dot_general | solution.py:41
  207.3 5.3 %fusion.61 = f32[3,1024]{1,0:T(4,128)S(1)} fusion(f32[]{:T(128)} %get-tuple-element.335, f32[1024]{0:T(1024)S(1)} %bitcast.49, f32[1024]{0:T(1024)S(1)} %bitcast.47, f32[1024]{0:T(1024)S(1)} %bitcast.48, f32[1024]{0:T(1024)S(1)} %bitcast.46, f32[1024]{0:T(1024)S(1)} %bitcast.50, f32[1024]{0:T(1024)S(1)} %bitcast.45, ...), kind=kOutput, calls=%fused_computation.19.clone.1 | convolution fusion | flops 54532096 | bytes 69645 | tf_op jit(solution)/shard_map/while/body/eval_jaxpr/dot_general | solution.py:41
  212.6 5.3 %fusion.61 = f32[3,1024]{1,0:T(4,128)S(1)} fusion(f32[]{:T(128)} %get-tuple-element.335, f32[1024]{0:T(1024)S(1)} %bitcast.49, f32[1024]{0:T(1024)S(1)} %bitcast.47, f32[1024]{0:T(1024)S(1)} %bitcast.48, f32[1024]{0:T(1024)S(1)} %bitcast.46, f32[1024]{0:T(1024)S(1)} %bitcast.50, f32[1024]{0:T(1024)S(1)} %bitcast.45, ...), kind=kOutput, calls=%fused_computation.19.clone.1 | convolution fusion | flops 54532096 | bytes 69645 | tf_op jit(solution)/shard_map/while/body/eval_jaxpr/dot_general | solution.py:41
  218.0 5.3 %fusion.61 = f32[3,1024]{1,0:T(4,128)S(1)} fusion(f32[]{:T(128)} %get-tuple-element.335, f32[1024]{0:T(1024)S(1)} %bitcast.49, f32[1024]{0:T(1024)S(1)} %bitcast.47, f32[1024]{0:T(1024)S(1)} %bitcast.48, f32[1024]{0:T(1024)S(1)} %bitcast.46, f32[1024]{0:T(1024)S(1)} %bitcast.50, f32[1024]{0:T(1024)S(1)} %bitcast.45, ...), kind=kOutput, calls=%fused_computation.19.clone.1 | convolution fusion | flops 54532096 | bytes 69645 | tf_op jit(solution)/shard_map/while/body/eval_jaxpr/dot_general | solution.py:41
  223.4 5.3 %fusion.61 = f32[3,1024]{1,0:T(4,128)S(1)} fusion(f32[]{:T(128)} %get-tuple-element.335, f32[1024]{0:T(1024)S(1)} %bitcast.49, f32[1024]{0:T(1024)S(1)} %bitcast.47, f32[1024]{0:T(1024)S(1)} %bitcast.48, f32[1024]{0:T(1024)S(1)} %bitcast.46, f32[1024]{0:T(1024)S(1)} %bitcast.50, f32[1024]{0:T(1024)S(1)} %bitcast.45, ...), kind=kOutput, calls=%fused_computation.19.clone.1 | convolution fusion | flops 54532096 | bytes 69645 | tf_op jit(solution)/shard_map/while/body/eval_jaxpr/dot_general | solution.py:41
  228.7 5.3 %fusion.61 = f32[3,1024]{1,0:T(4,128)S(1)} fusion(f32[]{:T(128)} %get-tuple-element.335, f32[1024]{0:T(1024)S(1)} %bitcast.49, f32[1024]{0:T(1024)S(1)} %bitcast.47, f32[1024]{0:T(1024)S(1)} %bitcast.48, f32[1024]{0:T(1024)S(1)} %bitcast.46, f32[1024]{0:T(1024)S(1)} %bitcast.50, f32[1024]{0:T(1024)S(1)} %bitcast.45, ...), kind=kOutput, calls=%fused_computation.19.clone.1 | convolution fusion | flops 54532096 | bytes 69645 | tf_op jit(solution)/shard_map/while/body/eval_jaxpr/dot_general | solution.py:41
  234.1 5.3 %fusion.61 = f32[3,1024]{1,0:T(4,128)S(1)} fusion(f32[]{:T(128)} %get-tuple-element.335, f32[1024]{0:T(1024)S(1)} %bitcast.49, f32[1024]{0:T(1024)S(1)} %bitcast.47, f32[1024]{0:T(1024)S(1)} %bitcast.48, f32[1024]{0:T(1024)S(1)} %bitcast.46, f32[1024]{0:T(1024)S(1)} %bitcast.50, f32[1024]{0:T(1024)S(1)} %bitcast.45, ...), kind=kOutput, calls=%fused_computation.19.clone.1 | convolution fusion | flops 54532096 | bytes 69645 | tf_op jit(solution)/shard_map/while/body/eval_jaxpr/dot_general | solution.py:41
  239.5 75.9 %psum.22 = f32[3]{0:T(128)S(1)} all-reduce(f32[3]{0:T(128)S(1)} %multiply_reduce_fusion), channel_id=1, replica_groups=mesh['blk'=8,'grp'=32] {'blk','grp'}, use_global_device_ids=true, to_apply=%region_5.0 | all-reduce | flops 3 | bytes 24 | tf_op jit(solution)/shard_map/psum | solution.py:81
  315.5 0.8 fusion.50
  316.3 42.5 %all_gather.3 = f32[6,32768]{1,0:T(8,128)S(1)} all-gather(f32[6,1024]{1,0:T(8,128)S(1)} %pad_maximum_fusion.1), channel_id=1, replica_groups=mesh['blk'=8,'grp'=32] {'grp'}, dimensions={1}, use_global_device_ids=true | all-gather | bytes 811008 | tf_op jit(solution)/shard_map/all_gather | solution.py:96
  358.8 26.1 %while.26 = (s32[]{:T(128)}, f32[3,1024]{1,0:T(4,128)S(1)}, s32[4]{0:T(128)S(1)}, f32[6,32768]{1,0:T(8,128)S(1)}, f32[3,1024]{1,0:T(4,128)S(1)}, /*index=5*/f32[...) while((s32[]{:T(128)}, f32[3,1024]{1,0:T(4,128)S(1)}, ...), condition=%wide.region_9.10_spmd.clone, body=%wide.region_8.9_spmd.clone.sunk | while | flops 54532104 | bytes 119037 | solution.py:102
  360.1 5.3 %fusion.64 = f32[3,1024]{1,0:T(4,128)S(1)} fusion(f32[]{:T(128)} %get-tuple-element.374, f32[1024]{0:T(1024)S(1)} %bitcast.55, f32[1024]{0:T(1024)S(1)} %bitcast.53, f32[1024]{0:T(1024)S(1)} %bitcast.54, f32[1024]{0:T(1024)S(1)} %bitcast.52, f32[1024]{0:T(1024)S(1)} %bitcast.56, f32[1024]{0:T(1024)S(1)} %bitcast.51, ...), kind=kOutput, calls=%fused_computation.44.clone.1 | convolution fusion | flops 54532096 | bytes 69645 | tf_op jit(solution)/shard_map/while/body/eval_jaxpr/dot_general | solution.py:92
  365.3 0.6 dynamic_slice.18
  366.6 5.3 %fusion.64 = f32[3,1024]{1,0:T(4,128)S(1)} fusion(f32[]{:T(128)} %get-tuple-element.374, f32[1024]{0:T(1024)S(1)} %bitcast.55, f32[1024]{0:T(1024)S(1)} %bitcast.53, f32[1024]{0:T(1024)S(1)} %bitcast.54, f32[1024]{0:T(1024)S(1)} %bitcast.52, f32[1024]{0:T(1024)S(1)} %bitcast.56, f32[1024]{0:T(1024)S(1)} %bitcast.51, ...), kind=kOutput, calls=%fused_computation.44.clone.1 | convolution fusion | flops 54532096 | bytes 69645 | tf_op jit(solution)/shard_map/while/body/eval_jaxpr/dot_general | solution.py:92
  373.1 5.3 %fusion.64 = f32[3,1024]{1,0:T(4,128)S(1)} fusion(f32[]{:T(128)} %get-tuple-element.374, f32[1024]{0:T(1024)S(1)} %bitcast.55, f32[1024]{0:T(1024)S(1)} %bitcast.53, f32[1024]{0:T(1024)S(1)} %bitcast.54, f32[1024]{0:T(1024)S(1)} %bitcast.52, f32[1024]{0:T(1024)S(1)} %bitcast.56, f32[1024]{0:T(1024)S(1)} %bitcast.51, ...), kind=kOutput, calls=%fused_computation.44.clone.1 | convolution fusion | flops 54532096 | bytes 69645 | tf_op jit(solution)/shard_map/while/body/eval_jaxpr/dot_general | solution.py:92
  379.6 5.3 %fusion.64 = f32[3,1024]{1,0:T(4,128)S(1)} fusion(f32[]{:T(128)} %get-tuple-element.374, f32[1024]{0:T(1024)S(1)} %bitcast.55, f32[1024]{0:T(1024)S(1)} %bitcast.53, f32[1024]{0:T(1024)S(1)} %bitcast.54, f32[1024]{0:T(1024)S(1)} %bitcast.52, f32[1024]{0:T(1024)S(1)} %bitcast.56, f32[1024]{0:T(1024)S(1)} %bitcast.51, ...), kind=kOutput, calls=%fused_computation.44.clone.1 | convolution fusion | flops 54532096 | bytes 69645 | tf_op jit(solution)/shard_map/while/body/eval_jaxpr/dot_general | solution.py:92
  384.9 73.3 %psum.23 = f32[3]{0:T(128)} all-reduce(f32[3]{0:T(128)S(1)} %get-tuple-element.194), channel_id=1, replica_groups=mesh['blk'=8,'grp'=32] {'blk','grp'}, use_global_device_ids=true, to_apply=%region_7.0 | all-reduce | flops 3 | bytes 24 | tf_op jit(solution)/shard_map/psum | solution.py:85
  (55 shorter events, 4.6 us)
Async XLA Ops:
  85.0 230.4 %copy-start.1 = (f32[3,1024]{1,0:T(4,128)}, f32[3,1024]{1,0:T(4,128)S(1)}, u32[]{:S(2)}) copy-start(f32[3,1024]{1,0:T(4,128)S(1)} %multiply_add_fusion.2) | copy-start | bytes 36868
  85.8 5.2 %collective-permute-start = (f32[6,1024]{1,0:T(8,128)S(1)}, f32[6,1024]{1,0:T(8,128)S(1)}, u32[]{:S(2)}, u32[]{:S(2)}) collective-permute-start(f32[6,1024]{1,0:T(8,128)S(1)} %pad_maximum_fusion.2), channel_id=1, source_target_pairs={{0,1},{1,2},{2,3},{3,4},{4,5},{5,6},{6,7},{7,8},{8,9},{9,10},{10,1... | collective-permute-start | bytes 73736 | tf_op jit(solution)/shard_map/ppermute | solution.py:16
  89.1 5.2 %collective-permute-start.1 = (f32[6,1024]{1,0:T(8,128)S(1)}, f32[6,1024]{1,0:T(8,128)S(1)}, u32[]{:S(2)}, u32[]{:S(2)}) collective-permute-start(f32[6,1024]{1,0:T(8,128)S(1)} %pad_maximum_fusion.2), channel_id=1, source_target_pairs={{1,0},{2,1},{3,2},{4,3},{5,4},{6,5},{7,6},{8,7},{9,8},{10,9},{11,1... | collective-permute-start | bytes 73736 | tf_op jit(solution)/shard_map/ppermute | solution.py:17
  95.1 15.4 %copy-start = (f32[3,1024]{1,0:T(4,128)S(1)}, f32[3,1024]{1,0:T(4,128)}, u32[]{:S(2)}) copy-start(f32[3,1024]{1,0:T(4,128)} %param.13) | copy-start | bytes 36868
  96.0 14.5 %all-to-all-start = ((f32[8,6,3072]{2,1,0:T(8,128)}), f32[8,6,3072]{2,1,0:T(8,128)S(1)}, u32[]{:S(2)}, u32[]{:S(2)}) async-start(f32[8,6,3072]{2,1,0:T(8,128)} %stack.2), calls=%async_computation | async-start | bytes 1572864 | tf_op jit(solution)/shard_map/all_to_all | solution.py:71
  110.5 128.9 %copy-start.5 = (f32[1024]{0:T(1024)S(1)}, f32[1024]{0:T(1024)}, u32[]{:S(2)}) copy-start(f32[1024]{0:T(1024)} %param.17) | copy-start | bytes 12292
  110.5 205.0 %copy-start.3 = (f32[3,1024]{1,0:T(4,128)S(1)}, f32[3,1024]{1,0:T(4,128)}, u32[]{:S(2)}) copy-start(f32[3,1024]{1,0:T(4,128)} %param.15) | copy-start | bytes 36868
  110.5 205.0 %copy-start.6 = (f32[3,1024]{1,0:T(4,128)S(1)}, f32[3,1024]{1,0:T(4,128)}, u32[]{:S(2)}) copy-start(f32[3,1024]{1,0:T(4,128)} %param.14) | copy-start | bytes 36868
  239.4 119.4 %copy-start.2 = (f32[3,1024]{1,0:T(4,128)S(1)}, f32[3,1024]{1,0:T(4,128)}, u32[]{:S(2)}) copy-start(f32[3,1024]{1,0:T(4,128)} %param.20) | copy-start | bytes 36868
  239.4 119.4 %copy-start.7 = (s32[1,4]{1,0:T(1,128)S(1)}, s32[1,4]{1,0:T(1,128)}, u32[]{:S(2)}) copy-start(s32[1,4]{1,0:T(1,128)} %param.21) | copy-start | bytes 52
  316.3 42.6 %copy-start.4 = (f32[3,1024]{1,0:T(4,128)}, f32[3,1024]{1,0:T(4,128)S(1)}, u32[]{:S(2)}) copy-start(f32[3,1024]{1,0:T(4,128)S(1)} %get-tuple-element.214) | copy-start | bytes 36868
  384.9 73.3 %copy-start.8 = (f32[3,1024]{1,0:T(4,128)}, f32[3,1024]{1,0:T(4,128)S(1)}, u32[]{:S(2)}) copy-start(f32[3,1024]{1,0:T(4,128)S(1)} %get-tuple-element.130) | copy-start | bytes 36868
